TPU v7x, 128 devices: a whole 4x4x4 slice. The times are simulated.
128 devices in a mesh: ctx: 8 (over x, y_hi), head: 16 (over y_lo, z, core).
Axes of the slice: x: 4, y: 4 (y_hi: 2, y_lo: 2; y = y_hi * 2 + y_lo), z: 4, core: 2. Of those that a mesh axis runs over, the one named last changes fastest.
Arguments:
- hidden_in: bfloat16 [8192, 5376], P(('ctx', 'head')), may hold values from -6 to 6
- pre_gain: float32 [5376], replicated, may hold values from 0.1 to 1.9
- w_query: bfloat16 [5376, 4096], P('ctx', 'head'), may hold values from -0.054554473 to 0.054554473, as said below
- w_key: bfloat16 [5376, 2048], P('ctx', 'head'), may hold values from -0.054554473 to 0.054554473, as said below
- value_weight: bfloat16 [5376, 2048], P('ctx', 'head'), may hold values from -0.078125 to 0.078125
- query_gain: float32 [128], replicated, may hold values from 0.6 to 7, as said below
- key_norm_gain: float32 [128], replicated, may hold values from 0.6 to 7, as said below
- w_output: bfloat16 [4096, 5376], P(('head', 'ctx')), may hold values from -0.09375 to 0.09375
- post_gain: float32 [5376], replicated, may hold values from 0.1 to 1.9
Outputs:
- layer_out: bfloat16 [8192, 5376], P(('ctx', 'head'))
Inputs may be any that keep to these rules, and one draw needn't show every extreme that they name: `w_query`: entries are normal draws clipped to 4 standard deviations, scaled by 5376 ** -0.5. `w_key`: entries are normal draws clipped to 4 standard deviations, scaled by 5376 ** -0.5. `query_gain`: positive gains. `key_norm_gain`: positive gains.
All inputs are finite; a program needn't handle non-finite values.
Results may differ from a plain program's by a relative error of at most 0.015.
The roundings to bfloat16 on the way count: a program that leaves them out, or rounds other values in their place, can miss the bound.
Values may be sent and summed in bfloat16 or wider, within the bound.
No kernel may reach another device: no remote copies, remote signals or barrier semaphores. Data moves between devices by JAX's collectives and lax.ppermute only.
A program may use at most 64 MiB of HBM per device.

v0:
```python
import jax
import jax.numpy as jnp
from jax import lax
from jax.sharding import PartitionSpec as P

HEAD_SIZE = 128
WINDOW_SPAN = 1024
norm_eps = 1e-06
query_scale = 168.0 ** (-0.5)
rope_base = 10000.0
mask_value = -1e30


def passed_along(shard, axis, by):
    count = lax.axis_size(axis)
    pairs = [(i, i + by) for i in range(count) if 0 <= i + by < count]
    return lax.ppermute(shard, axis, pairs)


def root_mean_scale(values, scaling):
    mean_sq = jnp.mean(values * values, axis=-1, keepdims=True)
    return values * lax.rsqrt(mean_sq + norm_eps) * scaling


def apply_rotary(values, token_places):
    full_width = values.shape[-1]
    half_width = full_width // 2
    frequency = rope_base ** (-jnp.arange(half_width, dtype=jnp.float32) * 2.0 / full_width)
    angles = token_places.astype(jnp.float32)[:, None] * frequency[None, :]
    cosine = jnp.cos(angles)[:, None, :]
    sine_part = jnp.sin(angles)[:, None, :]
    lower_half = values[..., :half_width]
    upper_half = values[..., half_width:]
    return jnp.concatenate(
        [
            lower_half * cosine - upper_half * sine_part,
            upper_half * cosine + lower_half * sine_part,
        ],
        axis=-1,
    )


def body(
    hidden_in,
    pre_gain,
    w_query,
    w_key,
    value_weight,
    query_gain,
    key_norm_gain,
    w_output,
    post_gain,
):
    own_rows = hidden_in.astype(jnp.float32)
    raw_rows = lax.all_gather(hidden_in, "head", axis=0, tiled=True)
    normed = root_mean_scale(raw_rows.astype(jnp.float32), pre_gain).astype(jnp.bfloat16)
    tok_count = normed.shape[0]

    def add_rows(weight_piece):
        return jnp.dot(normed, weight_piece, preferred_element_type=jnp.float32)

    query_raw = add_rows(lax.all_gather(w_query, "ctx", axis=0, tiled=True))
    key_unnormed = add_rows(lax.all_gather(w_key, "ctx", axis=0, tiled=True))
    value_unnormed = add_rows(lax.all_gather(value_weight, "ctx", axis=0, tiled=True))
    local_heads = w_query.shape[1] // HEAD_SIZE
    local_groups = w_key.shape[1] // HEAD_SIZE
    heads_per_group = local_heads // local_groups
    ctx_index = lax.axis_index("ctx")
    token_places = ctx_index * tok_count + jnp.arange(tok_count, dtype=jnp.int32)
    query_matrix = (
        apply_rotary(
            root_mean_scale(query_raw.reshape(tok_count, local_heads, HEAD_SIZE), query_gain),
            token_places,
        )
        * query_scale
    ).astype(jnp.bfloat16)
    projected_keys = apply_rotary(
        root_mean_scale(key_unnormed.reshape(tok_count, local_groups, HEAD_SIZE), key_norm_gain),
        token_places,
    ).astype(jnp.bfloat16)
    projected_values = value_unnormed.astype(jnp.bfloat16)
    key_value = jnp.stack(
        [projected_keys.reshape(tok_count, local_groups * HEAD_SIZE), projected_values]
    )
    pieces = [passed_along(key_value, "ctx", 1)]
    extended = jnp.concatenate(pieces + [key_value], axis=1)
    band_keys = extended[0].reshape(-1, local_groups, HEAD_SIZE)
    band_values = extended[1].reshape(-1, local_groups, HEAD_SIZE)
    block_rows = min(512, tok_count)
    grouped_queries = query_matrix.reshape(tok_count, local_groups, heads_per_group, HEAD_SIZE)
    outputs = []
    for block_index in range(tok_count // block_rows):
        first_row = block_index * block_rows
        query_block = grouped_queries[first_row : first_row + block_rows]
        key_block = band_keys[first_row : first_row + block_rows + WINDOW_SPAN]
        value_block = band_values[first_row : first_row + block_rows + WINDOW_SPAN]
        scores = jnp.einsum(
            "qjgd,kjd->jgqk", query_block, key_block, preferred_element_type=jnp.float32
        )
        query_spots = token_places[first_row : first_row + block_rows]
        key_spots = (
            ctx_index * tok_count
            - WINDOW_SPAN
            + first_row
            + jnp.arange(block_rows + WINDOW_SPAN, dtype=jnp.int32)
        )
        allowed = (
            (key_spots[None, :] <= query_spots[:, None])
            & (key_spots[None, :] > query_spots[:, None] - WINDOW_SPAN)
            & (key_spots[None, :] >= 0)
        )
        scores = jnp.where(allowed, scores, mask_value)
        row_max = jnp.max(scores, axis=-1, keepdims=True)
        weights = jnp.exp(scores - row_max)
        row_sum = jnp.sum(weights, axis=-1, keepdims=True)
        probabilities = (weights / row_sum).astype(jnp.bfloat16)
        mixed = jnp.einsum(
            "jgqk,kjd->qjgd", probabilities, value_block, preferred_element_type=jnp.float32
        )
        outputs.append(mixed.astype(jnp.bfloat16).reshape(block_rows, local_heads * HEAD_SIZE))
    attended = jnp.concatenate(outputs, axis=0)
    out_weight = lax.all_gather(w_output, "ctx", axis=0, tiled=True)
    partial_value = jnp.dot(attended, out_weight, preferred_element_type=jnp.float32).astype(
        jnp.bfloat16
    )
    summed = lax.psum_scatter(
        lax.optimization_barrier(partial_value).astype(jnp.float32).astype(jnp.bfloat16),
        "head",
        scatter_dimension=0,
        tiled=True,
    ).astype(jnp.float32)
    result = own_rows + root_mean_scale(summed, post_gain)
    return result.astype(jnp.bfloat16)


def solution(mesh):
    return jax.shard_map(
        body,
        mesh=mesh,
        in_specs=(
            P(("ctx", "head"), None),
            P(),
            P("ctx", "head"),
            P("ctx", "head"),
            P("ctx", "head"),
            P(),
            P(),
            P(("head", "ctx"), None),
            P(),
        ),
        out_specs=P(("ctx", "head"), None),
        check_vma=False,
    )
```

profile of v0, /device:TPU:0, one launch (start us, length us, event | category | flops | bytes accessed | tf_op | source)
XLA Modules:
  0.0 400.9 jit_solution(7037838070945432475)
XLA Ops:
  10.1 3.0 multiply_cosine_fusion
  13.1 1.8 and_and_fusion.1
  15.0 1.9 and_and_fusion
  16.8 59.2 %all-gather.6.cloned.1.call-done = bf16[1024,5376]{1,0:T(8,128)(2,1)} async-done(((bf16[64,5376]{1,0:T(8,128)(2,1)}), bf16[1024,5376]{1,0:T(8,128)(2,1)}) %all-gather.6.cloned.1.call-update) | async-done | bytes 11010064 | tf_op jit(solution)/shard_map/all_gather | solution.py:55
  76.0 6.5 %fusion = f32[1024]{0:T(1024)S(1)} fusion(bf16[1024,5376]{1,0:T(8,128)(2,1)} %all-gather.6.cloned.1.call-done), kind=kLoop, calls=%fused_computation.2 | loop fusion | flops 16514048 | bytes 11014144 | tf_op jit(solution)/shard_map/reduce_sum | solution.py:21
  83.3 6.0 %fusion.2 = bf16[1024,5376]{1,0:T(8,128)(2,1)} fusion(bf16[1024,5376]{1,0:T(8,128)(2,1)S(1)} %copy-done, f32[5376]{0:T(1024)S(1)} %copy-done.6, f32[1024]{0:T(1024)S(1)} %add_rsqrt_fusion.2), kind=kLoop, calls=%fused_computation.4 | loop fusion | flops 22020096 | bytes 22045696 | tf_op jit(solution)/shard_map/convert_element_type | solution.py:56
  89.2 39.5 %all-gather.8.cloned.1.call-done = bf16[5376,128]{1,0:T(8,128)(2,1)} async-done(((bf16[672,128]{1,0:T(8,128)(2,1)}), bf16[5376,128]{1,0:T(8,128)(2,1)}) %all-gather.8.cloned.1.call-update) | async-done | bytes 1376272 | tf_op jit(solution)/shard_map/all_gather | solution.py:63
  128.7 8.2 %multiply_reduce_fusion.1 = (f32[1024]{0:T(1024)S(1)}, f32[1024,128]{0,1:T(8,128)S(1)}) fusion(bf16[1024,5376]{1,0:T(8,128)(2,1)} %fusion.2, bf16[5376,128]{1,0:T(8,128)(2,1)} %all-gather.8.cloned.1.call-done), kind=kOutput, calls=%fused_computation.46 | convolution fusion | flops 1409547264 | bytes 12914688 | tf_op jit(solution)/shard_map/dot_general | solution.py:60
  138.2 41.1 %all-gather.10.cloned.1.call-done = bf16[5376,128]{1,0:T(8,128)(2,1)} async-done(((bf16[672,128]{1,0:T(8,128)(2,1)}), bf16[5376,128]{1,0:T(8,128)(2,1)}) %all-gather.10.cloned.1.call-update) | async-done | bytes 1376272 | tf_op jit(solution)/shard_map/all_gather | solution.py:64
  179.3 8.2 %fusion.21 = bf16[1,1024,128]{1,2,0:T(8,128)(2,1)S(1)} fusion(bf16[1024,5376]{1,0:T(8,128)(2,1)} %fusion.2, bf16[5376,128]{1,0:T(8,128)(2,1)} %all-gather.10.cloned.1.call-done), kind=kOutput, calls=%fused_computation.31 | convolution fusion | flops 1409417216 | bytes 12648448 | tf_op jit(solution)/shard_map/dot_general | solution.py:60
  187.6 3.4 collective-permute-start
  191.0 52.1 %all-gather.12.cloned.1.call-done = bf16[5376,256]{1,0:T(8,128)(2,1)} async-done(((bf16[672,256]{1,0:T(8,128)(2,1)}), bf16[5376,256]{1,0:T(8,128)(2,1)}) %all-gather.12.cloned.1.call-update) | async-done | bytes 2752528 | tf_op jit(solution)/shard_map/all_gather | solution.py:62
  243.1 9.0 %multiply_reduce_fusion = (f32[1024,2]{0,1:T(2,128)S(1)}, f32[1024,256]{0,1:T(8,128)}) fusion(bf16[1024,5376]{1,0:T(8,128)(2,1)} %fusion.2, bf16[5376,256]{1,0:T(8,128)(2,1)} %all-gather.12.cloned.1.call-done), kind=kOutput, calls=%fused_computation.38 | convolution fusion | flops 2819094528 | bytes 14819328 | tf_op jit(solution)/shard_map/dot_general | solution.py:60
  252.1 1.6 copy.11
  256.1 1.3 fusion.3
  257.4 1.3 fusion.4
  258.7 1.2 fusion.5
  261.2 2.0 fusion.15
  263.2 2.2 fusion.18
  265.4 38.4 %all-gather.14.cloned.1.call-done = bf16[256,5376]{1,0:T(8,128)(2,1)} async-done(((bf16[32,5376]{1,0:T(8,128)(2,1)}), bf16[256,5376]{1,0:T(8,128)(2,1)}) %all-gather.14.cloned.1.call-update) | async-done | bytes 2752528 | tf_op jit(solution)/shard_map/all_gather | solution.py:122
  303.9 7.6 %convolution_convert_fusion = bf16[1024,5376]{1,0:T(8,128)(2,1)} fusion(bf16[256,5376]{1,0:T(8,128)(2,1)} %all-gather.14.cloned.1.call-done, bf16[512,256]{0,1:T(8,128)(2,1)S(1)} %bitcast.95, bf16[512,256]{0,1:T(8,128)(2,1)S(1)} %bitcast.94), kind=kOutput, calls=%fused_computation.5 | convolution fusion | flops 2825125888 | bytes 14286848 | tf_op jit(solution)/shard_map/dot_general | solution.py:123
  311.5 78.9 %reduce-scatter.2.cloned.1.call-done = bf16[64,5376]{1,0:T(8,128)(2,1)} async-done(((bf16[1024,5376]{1,0:T(8,128)(2,1)}), bf16[64,5376]{1,0:T(8,128)(2,1)}) %reduce-scatter.2.cloned.1.call-update) | async-done | bytes 688144 | tf_op jit(solution)/shard_map/reduce_scatter | solution.py:126
  390.4 1.3 fusion.11
  391.8 2.3 fusion.14
  (52 shorter events, 9.1 us)
Async XLA Ops:
  6.5 69.5 %all-gather.6.cloned.1.call-start = ((), (), s32[]{:S(2)}) async-start(), calls=%async_computation.1 | async-start | bytes 11698176 | tf_op jit(solution)/shard_map/all_gather | solution.py:55
  7.3 121.5 %all-gather.8.cloned.1.call-start = ((), (), s32[]{:S(2)}) async-start(), calls=%async_computation.2 | async-start | bytes 1548288 | tf_op jit(solution)/shard_map/all_gather | solution.py:63
  8.0 171.3 %all-gather.10.cloned.1.call-start = ((), (), s32[]{:S(2)}) async-start(), calls=%async_computation.3 | async-start | bytes 1548288 | tf_op jit(solution)/shard_map/all_gather | solution.py:64
  8.7 234.4 %all-gather.12.cloned.1.call-start = ((), (), s32[]{:S(2)}) async-start(), calls=%async_computation.4 | async-start | bytes 3096576 | tf_op jit(solution)/shard_map/all_gather | solution.py:62
  9.3 294.5 %all-gather.14.cloned.1.call-start = ((), (), s32[]{:S(2)}) async-start(), calls=%async_computation.5 | async-start | bytes 3096576 | tf_op jit(solution)/shard_map/all_gather | solution.py:122
  9.9 380.5 %reduce-scatter.2.cloned.1.call-start = ((), (), s32[]{:S(2)}) async-start(), calls=%async_computation.6 | async-start | bytes 11698176 | tf_op jit(solution)/shard_map/reduce_scatter | solution.py:126
  13.1 69.4 %copy-start.6 = (f32[5376]{0:T(1024)S(1)}, f32[5376]{0:T(1024)}, u32[]{:S(2)}) copy-start(f32[5376]{0:T(1024)} %param.10) | copy-start | bytes 64516
  76.0 7.3 %copy-start = (bf16[1024,5376]{1,0:T(8,128)(2,1)S(1)}, bf16[1024,5376]{1,0:T(8,128)(2,1)}, u32[]{:S(2)}) copy-start(bf16[1024,5376]{1,0:T(8,128)(2,1)} %all-gather.6.cloned.1.call-done) | copy-start | bytes 33030148
  89.2 47.7 %copy-start.8 = (f32[128]{0:T(128)S(1)}, f32[128]{0:T(128)}, u32[]{:S(2)}) copy-start(f32[128]{0:T(128)} %param.15) | copy-start | bytes 1540
  187.6 66.1 %copy-start.9 = (f32[128]{0:T(128)S(1)}, f32[128]{0:T(128)}, u32[]{:S(2)}) copy-start(f32[128]{0:T(128)} %param.14) | copy-start | bytes 1540
  187.6 66.5 %copy-start.4 = (f32[1024,64]{1,0:T(8,128)S(1)}, f32[1024,64]{1,0:T(8,128)}, u32[]{:S(2)}) copy-start(f32[1024,64]{1,0:T(8,128)} %get-tuple-element.9) | copy-start | bytes 786436
  187.6 66.5 %copy-start.5 = (f32[1024,64]{1,0:T(8,128)S(1)}, f32[1024,64]{1,0:T(8,128)}, u32[]{:S(2)}) copy-start(f32[1024,64]{1,0:T(8,128)} %get-tuple-element.10) | copy-start | bytes 786436
  187.6 67.4 %collective-permute-start = (bf16[2,1024,128]{1,2,0:T(8,128)(2,1)S(1)}, bf16[2,1024,128]{1,2,0:T(8,128)(2,1)}, u32[]{:S(2)}, u32[]{:S(2)}) collective-permute-start(bf16[2,1024,128]{1,2,0:T(8,128)(2,1)S(1)} %pad_maximum_fusion), channel_id=1, source_target_pairs={{0,16},{16,32},{32,48},{48,64},{64,80},{80,96},{96,112},{1,17},{17... | collective-permute-start | bytes 1572872 | tf_op jit(solution)/shard_map/ppermute | solution.py:17
  253.7 2.4 copy-start.1
  254.6 2.8 copy-start.2
  311.5 80.3 %copy-start.3 = (bf16[64,5376]{1,0:T(8,128)(2,1)S(1)}, bf16[64,5376]{1,0:T(8,128)(2,1)}, u32[]{:S(2)}) copy-start(bf16[64,5376]{1,0:T(8,128)(2,1)} %param.9) | copy-start | bytes 2064388
  311.5 80.3 %copy-start.7 = (f32[5376]{0:T(1024)S(1)}, f32[5376]{0:T(1024)}, u32[]{:S(2)}) copy-start(f32[5376]{0:T(1024)} %param.17) | copy-start | bytes 64516
Sparse Core Ops, SparseCore 0:
  9.0 66.9 all-gather.5
  78.3 50.3 all-gather.7
  131.0 48.2 all-gather.9
  181.5 61.6 all-gather.11
  245.3 58.5 all-gather.13
  311.7 78.7 reduce-scatter.1
where the time goes:
time: 401 us
  waiting for transfers between devices  312 us (78%)
  matrix products  39.9 us (10%)
  other arithmetic  28.9 us (7%)
  between operations  13.8 us (3%)
    reduce_scatter x1, waiting for transfers between devices, body(): lax.psum_scatter(lax.optimization_barrier(partial_value).astype(jnp.float...  78.9 us
    all_gather x1, waiting for transfers between devices, body(): raw_rows = lax.all_gather(hidden_in, 'head', axis=0, tiled=True)  59.2 us
    all_gather x1, waiting for transfers between devices, body(): query_raw = add_rows(lax.all_gather(w_query, 'ctx', axis=0, tiled=True))  52.1 us
    all_gather x1, waiting for transfers between devices, body(): lax.all_gather(value_weight, 'ctx', axis=0, tiled=True)  41.1 us
    all_gather x1, waiting for transfers between devices, body(): key_unnormed = add_rows(lax.all_gather(w_key, 'ctx', axis=0, tiled=True))  39.5 us
    all_gather x1, waiting for transfers between devices, body(): out_weight = lax.all_gather(w_output, 'ctx', axis=0, tiled=True)  38.4 us
    dot_general x3, matrix products, add_rows(): return jnp.dot(normed, weight_piece, preferred_element_type=jnp.float32)  25.4 us
  transfers between devices with their start and end apart: 7, of which 6 were waited for; matrix products, arithmetic and copies ran while one was open for 15% of the time, Pallas kernels for 0%

commit v1 on v0

--- a/solution.py
+++ b/solution.py
@@ -60,7 +60,11 @@
         return jnp.dot(normed, weight_piece, preferred_element_type=jnp.float32)
 
     query_raw = add_rows(lax.all_gather(w_query, "ctx", axis=0, tiled=True))
-    key_unnormed = add_rows(lax.all_gather(w_key, "ctx", axis=0, tiled=True))
+    key_unnormed = add_rows(
+        jnp.concatenate(
+            lax.all_to_all(jnp.stack([w_key] * lax.axis_size("ctx")), "ctx", 0, 0), axis=0
+        )
+    )
     value_unnormed = add_rows(lax.all_gather(value_weight, "ctx", axis=0, tiled=True))
     local_heads = w_query.shape[1] // HEAD_SIZE
     local_groups = w_key.shape[1] // HEAD_SIZE

time: 401 us -> 364 us (0.908)
  waiting for transfers between devices: 312 us -> 266 us
  starting transfers between devices: 3.56 us -> 10.6 us
    all_gather x1 -> x0, waiting for transfers between devices: 39.5 us -> none  [body(): key_unnormed = add_rows(lax.all_gather(w_key, 'ctx', axis=0, tiled=True))]
    all_gather x1, waiting for transfers between devices: 41.1 us -> 31.9 us  [body(): lax.all_gather(value_weight, 'ctx', axis=0, tiled=True)]
    all_to_all x0 -> x1, starting transfers between devices: none -> 7.04 us  [body(): lax.all_to_all(jnp.stack([w_key] * lax.axis_size('ctx')), 'ctx', 0, 0)]
  transfers between devices with their start and end apart: 7 -> 7, of which waited for: 6 -> 5; matrix products, arithmetic and copies ran while one was open for 15% -> 17% of each run, Pallas kernels for 0% -> 0%
where the time goes in v1:
time: 364 us; the launch traced here: 363 us
  waiting for transfers between devices  266 us (73%)
  matrix products  40 us (11%)
  other arithmetic  29 us (8%)
  between operations  13.4 us (4%)
  starting transfers between devices  10.6 us (3%)
  local copies, waits for them, and re-layouts  4.56 us (1%)
    reduce_scatter x1, waiting for transfers between devices, body(): lax.psum_scatter(lax.optimization_barrier(partial_value).astype(jnp.float...  78.9 us
    all_gather x1, waiting for transfers between devices, body(): raw_rows = lax.all_gather(hidden_in, 'head', axis=0, tiled=True)  61.8 us
    all_gather x1, waiting for transfers between devices, body(): query_raw = add_rows(lax.all_gather(w_query, 'ctx', axis=0, tiled=True))  52.2 us
    all_gather x1, waiting for transfers between devices, body(): out_weight = lax.all_gather(w_output, 'ctx', axis=0, tiled=True)  38.5 us
    all_gather x1, waiting for transfers between devices, body(): lax.all_gather(value_weight, 'ctx', axis=0, tiled=True)  31.9 us
    dot_general x3, matrix products, add_rows(): return jnp.dot(normed, weight_piece, preferred_element_type=jnp.float32)  25.6 us
    reduce_sum x2, other arithmetic, root_mean_scale(): mean_sq = jnp.mean(values * values, axis=-1, keepdims=True)  7.81 us
    dot_general x1, matrix products, body(): jnp.dot(attended, out_weight, preferred_element_type=jnp.float32)  7.65 us
  transfers between devices with their start and end apart: 7, of which 5 were waited for; matrix products, arithmetic and copies ran while one was open for 17% of the time, Pallas kernels for 0%

profile of v1, /device:TPU:0, one launch (start us, length us, event | category | flops | bytes accessed | tf_op | source)
XLA Modules:
  0.0 363.4 jit_solution(10609285395235612970)
XLA Ops:
  8.7 2.2 stack.6
  10.9 7.0 %all-to-all-start = ((bf16[8,672,128]{2,1,0:T(8,128)(2,1)}), bf16[8,672,128]{2,1,0:T(8,128)(2,1)}, u32[]{:S(2)}, u32[]{:S(2)}) async-start(bf16[8,672,128]{2,1,0:T(8,128)(2,1)} %stack.6), calls=%async_computation | async-start | bytes 2752512 | tf_op jit(solution)/shard_map/all_to_all | solution.py:65
  18.7 3.1 multiply_cosine_fusion
  21.8 1.8 and_and_fusion.1
  23.6 1.9 and_and_fusion
  25.5 61.8 %all-gather.5.cloned.1.call-done = bf16[1024,5376]{1,0:T(8,128)(2,1)} async-done(((bf16[64,5376]{1,0:T(8,128)(2,1)}), bf16[1024,5376]{1,0:T(8,128)(2,1)}) %all-gather.5.cloned.1.call-update) | async-done | bytes 11010064 | tf_op jit(solution)/shard_map/all_gather | solution.py:55
  87.2 6.5 %fusion = f32[1024]{0:T(1024)S(1)} fusion(bf16[1024,5376]{1,0:T(8,128)(2,1)} %all-gather.5.cloned.1.call-done), kind=kLoop, calls=%fused_computation.2 | loop fusion | flops 16514048 | bytes 11014144 | tf_op jit(solution)/shard_map/reduce_sum | solution.py:21
  94.5 6.0 %fusion.2 = bf16[1024,5376]{1,0:T(8,128)(2,1)} fusion(bf16[1024,5376]{1,0:T(8,128)(2,1)S(1)} %copy-done, f32[5376]{0:T(1024)S(1)} %copy-done.6, f32[1024]{0:T(1024)S(1)} %add_rsqrt_fusion.2), kind=kLoop, calls=%fused_computation.4 | loop fusion | flops 22020096 | bytes 22045696 | tf_op jit(solution)/shard_map/convert_element_type | solution.py:56
  100.5 8.4 %multiply_reduce_fusion.1 = (f32[1024]{0:T(1024)S(1)}, f32[1024,128]{0,1:T(8,128)S(1)}) fusion(bf16[1024,5376]{1,0:T(8,128)(2,1)} %fusion.2, bf16[5376,128]{1,0:T(8,128)(2,1)} %bitcast), kind=kOutput, calls=%fused_computation.46 | convolution fusion | flops 1409547264 | bytes 12914688 | tf_op jit(solution)/shard_map/dot_general | solution.py:60
  110.2 31.9 %all-gather.7.cloned.1.call-done = bf16[5376,128]{1,0:T(8,128)(2,1)} async-done(((bf16[672,128]{1,0:T(8,128)(2,1)}), bf16[5376,128]{1,0:T(8,128)(2,1)}) %all-gather.7.cloned.1.call-update) | async-done | bytes 1376272 | tf_op jit(solution)/shard_map/all_gather | solution.py:68
  142.1 8.2 %fusion.21 = bf16[1,1024,128]{1,2,0:T(8,128)(2,1)S(1)} fusion(bf16[1024,5376]{1,0:T(8,128)(2,1)} %fusion.2, bf16[5376,128]{1,0:T(8,128)(2,1)} %all-gather.7.cloned.1.call-done), kind=kOutput, calls=%fused_computation.31 | convolution fusion | flops 1409417216 | bytes 12648448 | tf_op jit(solution)/shard_map/dot_general | solution.py:60
  150.4 3.4 collective-permute-start
  153.7 52.2 %all-gather.9.cloned.1.call-done = bf16[5376,256]{1,0:T(8,128)(2,1)} async-done(((bf16[672,256]{1,0:T(8,128)(2,1)}), bf16[5376,256]{1,0:T(8,128)(2,1)}) %all-gather.9.cloned.1.call-update) | async-done | bytes 2752528 | tf_op jit(solution)/shard_map/all_gather | solution.py:62
  206.0 9.0 %multiply_reduce_fusion = (f32[1024,2]{0,1:T(2,128)S(1)}, f32[1024,256]{0,1:T(8,128)}) fusion(bf16[1024,5376]{1,0:T(8,128)(2,1)} %fusion.2, bf16[5376,256]{1,0:T(8,128)(2,1)} %all-gather.9.cloned.1.call-done), kind=kOutput, calls=%fused_computation.38 | convolution fusion | flops 2819094528 | bytes 14819328 | tf_op jit(solution)/shard_map/dot_general | solution.py:60
  214.9 1.6 copy.11
  218.9 1.3 fusion.3
  220.2 1.3 fusion.4
  224.0 2.0 fusion.15
  226.0 2.2 fusion.18
  228.2 38.5 %all-gather.11.cloned.1.call-done = bf16[256,5376]{1,0:T(8,128)(2,1)} async-done(((bf16[32,5376]{1,0:T(8,128)(2,1)}), bf16[256,5376]{1,0:T(8,128)(2,1)}) %all-gather.11.cloned.1.call-update) | async-done | bytes 2752528 | tf_op jit(solution)/shard_map/all_gather | solution.py:126
  266.7 7.6 %convolution_convert_fusion = bf16[1024,5376]{1,0:T(8,128)(2,1)} fusion(bf16[256,5376]{1,0:T(8,128)(2,1)} %all-gather.11.cloned.1.call-done, bf16[512,256]{0,1:T(8,128)(2,1)S(1)} %bitcast.96, bf16[512,256]{0,1:T(8,128)(2,1)S(1)} %bitcast.95), kind=kOutput, calls=%fused_computation.5 | convolution fusion | flops 2825125888 | bytes 14286848 | tf_op jit(solution)/shard_map/dot_general | solution.py:127
  274.4 78.9 %reduce-scatter.2.cloned.1.call-done = bf16[64,5376]{1,0:T(8,128)(2,1)} async-done(((bf16[1024,5376]{1,0:T(8,128)(2,1)}), bf16[64,5376]{1,0:T(8,128)(2,1)}) %reduce-scatter.2.cloned.1.call-update) | async-done | bytes 688144 | tf_op jit(solution)/shard_map/reduce_scatter | solution.py:130
  353.3 1.3 fusion.11
  354.6 2.3 fusion.14
  (52 shorter events, 9.8 us)
Async XLA Ops:
  6.5 80.7 %all-gather.5.cloned.1.call-start = ((), (), s32[]{:S(2)}) async-start(), calls=%async_computation.2 | async-start | bytes 11698176 | tf_op jit(solution)/shard_map/all_gather | solution.py:55
  7.3 134.8 %all-gather.7.cloned.1.call-start = ((), (), s32[]{:S(2)}) async-start(), calls=%async_computation.3 | async-start | bytes 1548288 | tf_op jit(solution)/shard_map/all_gather | solution.py:68
  8.0 198.0 %all-gather.9.cloned.1.call-start = ((), (), s32[]{:S(2)}) async-start(), calls=%async_computation.4 | async-start | bytes 3096576 | tf_op jit(solution)/shard_map/all_gather | solution.py:62
  10.9 89.5 %all-to-all-start = ((bf16[8,672,128]{2,1,0:T(8,128)(2,1)}), bf16[8,672,128]{2,1,0:T(8,128)(2,1)}, u32[]{:S(2)}, u32[]{:S(2)}) async-start(bf16[8,672,128]{2,1,0:T(8,128)(2,1)} %stack.6), calls=%async_computation | async-start | bytes 2752512 | tf_op jit(solution)/shard_map/all_to_all | solution.py:65
  18.0 248.7 %all-gather.11.cloned.1.call-start = ((), (), s32[]{:S(2)}) async-start(), calls=%async_computation.5 | async-start | bytes 3096576 | tf_op jit(solution)/shard_map/all_gather | solution.py:126
  18.6 334.7 %reduce-scatter.2.cloned.1.call-start = ((), (), s32[]{:S(2)}) async-start(), calls=%async_computation.6 | async-start | bytes 11698176 | tf_op jit(solution)/shard_map/reduce_scatter | solution.py:130
  21.8 72.0 %copy-start.6 = (f32[5376]{0:T(1024)S(1)}, f32[5376]{0:T(1024)}, u32[]{:S(2)}) copy-start(f32[5376]{0:T(1024)} %param.10) | copy-start | bytes 64516
  87.2 7.3 %copy-start = (bf16[1024,5376]{1,0:T(8,128)(2,1)S(1)}, bf16[1024,5376]{1,0:T(8,128)(2,1)}, u32[]{:S(2)}) copy-start(bf16[1024,5376]{1,0:T(8,128)(2,1)} %all-gather.5.cloned.1.call-done) | copy-start | bytes 33030148
  100.5 8.4 %copy-start.8 = (f32[128]{0:T(128)S(1)}, f32[128]{0:T(128)}, u32[]{:S(2)}) copy-start(f32[128]{0:T(128)} %param.15) | copy-start | bytes 1540
  150.3 66.2 %copy-start.9 = (f32[128]{0:T(128)S(1)}, f32[128]{0:T(128)}, u32[]{:S(2)}) copy-start(f32[128]{0:T(128)} %param.14) | copy-start | bytes 1540
  150.4 66.5 %copy-start.4 = (f32[1024,64]{1,0:T(8,128)S(1)}, f32[1024,64]{1,0:T(8,128)}, u32[]{:S(2)}) copy-start(f32[1024,64]{1,0:T(8,128)} %get-tuple-element.9) | copy-start | bytes 786436
  150.4 66.5 %copy-start.5 = (f32[1024,64]{1,0:T(8,128)S(1)}, f32[1024,64]{1,0:T(8,128)}, u32[]{:S(2)}) copy-start(f32[1024,64]{1,0:T(8,128)} %get-tuple-element.10) | copy-start | bytes 786436
  150.4 67.4 %collective-permute-start = (bf16[2,1024,128]{1,2,0:T(8,128)(2,1)S(1)}, bf16[2,1024,128]{1,2,0:T(8,128)(2,1)}, u32[]{:S(2)}, u32[]{:S(2)}) collective-permute-start(bf16[2,1024,128]{1,2,0:T(8,128)(2,1)S(1)} %pad_maximum_fusion), channel_id=1, source_target_pairs={{0,16},{16,32},{32,48},{48,64},{64,80},{80,96},{96,112},{1,17},{17... | collective-permute-start | bytes 1572872 | tf_op jit(solution)/shard_map/ppermute | solution.py:17
  216.5 2.4 copy-start.1
  217.4 2.8 copy-start.2
  274.4 80.3 %copy-start.3 = (bf16[64,5376]{1,0:T(8,128)(2,1)S(1)}, bf16[64,5376]{1,0:T(8,128)(2,1)}, u32[]{:S(2)}) copy-start(bf16[64,5376]{1,0:T(8,128)(2,1)} %param.9) | copy-start | bytes 2064388
  274.4 80.3 %copy-start.7 = (f32[5376]{0:T(1024)S(1)}, f32[5376]{0:T(1024)}, u32[]{:S(2)}) copy-start(f32[5376]{0:T(1024)} %param.17) | copy-start | bytes 64516
Sparse Core Ops, SparseCore 0:
  9.0 78.1 all-gather.4
  89.6 52.4 all-gather.6
  144.4 61.5 all-gather.8
  208.1 58.5 all-gather.10
  274.5 78.7 reduce-scatter.1
